TPU v7x, 32 devices: a whole 2x2x4 slice. The times are simulated.
32 devices in a mesh: seq: 8 (over z, x), exp: 4 (over y, core).
Axes of the slice: x: 2, y: 2, z: 4, core: 2. Of those that a mesh axis runs over, the one named last changes fastest.
Arguments:
- hidden_in: bfloat16 [2048, 1536], P('seq'), may hold values from -6 to 6
- attn_gain: float32 [1536], replicated, may hold values from 0.1 to 1.9
- q_weight: bfloat16 [1536, 1536], P(None, 'exp'), may hold values from -1.25 to 1.25
- k_weight: bfloat16 [1536, 512], P(None, 'exp'), may hold values from -0.625 to 0.625
- v_weight: bfloat16 [1536, 512], P(None, 'exp'), may hold values from -0.15625 to 0.15625
- o_weight: bfloat16 [1536, 1536], P('exp'), may hold values from -0.15625 to 0.15625
- cache_kv: bfloat16 [4096, 1024], P('seq', 'exp'), may hold values from -216 to 216
- moe_gain: float32 [1536], replicated, may hold values from 0.1 to 1.9
- expert_in: bfloat16 [32, 1536, 1024], P('seq'), may hold values from -0.15625 to 0.15625
- expert_out: bfloat16 [32, 512, 1536], P('seq'), may hold values from -0.25 to 0.25
- routes: int32 [2048, 8], P(('seq', 'exp')), may hold values from 0 to 31, all different within a row; in each aligned block of 64 rows (0 to 63, 64 to 127, ...) at most 32 rows name the same one
- route_prob: float32 [2048, 8], P(('seq', 'exp')), may hold values from 0.05 to 1
- page_slot: int32 [256], replicated, may hold values from 0 to 31, as said below
Outputs:
- hidden_out: bfloat16 [2048, 1536], P(('seq', 'exp'))
- decode_pages: bfloat16 [256, 8, 2, 512], P('seq', 'exp')
Inputs may be any that keep to these rules, and one draw needn't show every extreme that they name: `routes`: in each aligned block of 64 rows (the rows of one device) no expert is named by more than 32 rows; a row names 8 different experts. `page_slot`: for each r, the 32 blocks b with b mod (8) == r have different slots.
All inputs are finite; a program needn't handle non-finite values.
Results may differ from a plain program's by a relative error of at most 0.0074.
Values may be sent and summed in bfloat16 or wider, within the bound.
No kernel may reach another device: no remote copies, remote signals or barrier semaphores. Data moves between devices by JAX's collectives and lax.ppermute only.
A program may use at most 128 MiB of HBM per device.

v0:
```python
import math
import jax
import jax.numpy as jnp
from jax import lax
from jax.sharding import PartitionSpec as P

HEADS = 24
KV_HEADS = 8
HEAD_DIM = 64
EXPERTS = 32
PAGE = 8
norm_epsilon = 1e-06
attention_scale = 0.015625
residual_scale = 0.22
masked_score = -1e30


def rms_norm(values, gain_row):
    widened = values.astype(jnp.float32)
    spread = lax.rsqrt(jnp.mean(widened * widened, axis=-1, keepdims=True) + norm_epsilon)
    return (widened * spread * gain_row).astype(jnp.bfloat16)


def attend_block(carried, query_heads, visible, key_rows, value_rows):
    best_old, total_old, summed_old = carried
    scores = (
        jnp.einsum("tkgd,nkd->kgtn", query_heads, key_rows, preferred_element_type=jnp.float32)
        * attention_scale
    )
    scores = jnp.where(visible, scores, masked_score)
    best_new = jnp.maximum(best_old, jnp.max(scores, axis=-1))
    weights = jnp.where(visible, jnp.exp(scores - best_new[..., None]), 0.0)
    factor = jnp.exp(best_old - best_new)
    total_new = total_old * factor + jnp.sum(weights, axis=-1)
    summed_new = summed_old * factor[..., None] + jnp.einsum(
        "kgtn,nkd->kgtd",
        weights.astype(jnp.bfloat16),
        value_rows,
        preferred_element_type=jnp.float32,
    )
    return (best_new, total_new, summed_new)


def block_size(piece_rows):
    return math.gcd(piece_rows, 512)


def body(
    hidden_in,
    attn_gain,
    q_weight,
    k_weight,
    v_weight,
    o_weight,
    cache_kv,
    moe_gain,
    expert_in,
    expert_out,
    routes,
    route_prob,
    page_slot,
):
    seq_count = lax.axis_size("seq")
    seq_index = lax.axis_index("seq")
    exp_index = lax.axis_index("exp")
    tokens_here = hidden_in.shape[0]
    head_dim = HEAD_DIM
    kv_local = k_weight.shape[1] // head_dim
    group_size = HEADS // KV_HEADS
    prompt_len = tokens_here * seq_count // 2
    first_row = seq_index * tokens_here
    query_rows = first_row + jnp.arange(tokens_here, dtype=jnp.int32)
    query_second = query_rows >= prompt_len
    holds_first = first_row < prompt_len
    normed = rms_norm(hidden_in, attn_gain)
    queries = jnp.dot(normed, q_weight, preferred_element_type=jnp.float32).astype(jnp.bfloat16)
    keys_new = jnp.dot(normed, k_weight, preferred_element_type=jnp.float32).astype(jnp.bfloat16)
    values_new = jnp.dot(normed, v_weight, preferred_element_type=jnp.float32).astype(jnp.bfloat16)
    pair_width = 2 * kv_local * head_dim
    pairs_new = jnp.stack(
        [
            keys_new.reshape(tokens_here, kv_local, head_dim),
            values_new.reshape(tokens_here, kv_local, head_dim),
        ],
        axis=2,
    ).reshape(tokens_here, pair_width)
    query_heads = queries.reshape(tokens_here, kv_local, group_size, head_dim)
    cache_lines = cache_kv.reshape(tokens_here, -1)
    blocks_here = tokens_here // PAGE
    rounds = blocks_here // seq_count
    outgoing = pairs_new.reshape(rounds, seq_count, PAGE * pair_width)
    received = lax.all_to_all(outgoing, "seq", split_axis=1, concat_axis=1, tiled=True)
    block_ids = (
        jnp.arange(seq_count, dtype=jnp.int32)[None, :] * blocks_here
        + jnp.arange(rounds, dtype=jnp.int32)[:, None] * seq_count
        + seq_index
    ).reshape(-1)
    table_ids = jnp.arange(page_slot.shape[0], dtype=jnp.int32)
    page_slots = jnp.sum(
        jnp.where(block_ids[:, None] == table_ids[None, :], page_slot[None, :], 0), axis=1
    )
    local_pages = (
        jnp.zeros((blocks_here, PAGE * pair_width), jnp.bfloat16)
        .at[page_slots]
        .set(received.reshape(blocks_here, -1))
    )
    page_rows = local_pages.reshape(blocks_here, PAGE, kv_local, 2, head_dim).transpose(
        0, 2, 3, 1, 4
    )
    page_rows = page_rows.reshape(blocks_here, kv_local, 2, PAGE * head_dim)
    start_state = (
        jnp.full((kv_local, group_size, tokens_here), masked_score, jnp.float32),
        jnp.zeros((kv_local, group_size, tokens_here), jnp.float32),
        jnp.zeros((kv_local, group_size, tokens_here, head_dim), jnp.float32),
    )

    def new_keys_part(carried, new_block, key_first):
        width_rows = new_block.shape[0]
        key_rows = key_first + jnp.arange(width_rows, dtype=jnp.int32)
        visible = ((key_rows >= prompt_len)[None, :] == query_second[:, None]) & (
            key_rows[None, :] <= query_rows[:, None]
        )
        split_pairs = new_block.reshape(width_rows, kv_local, 2, head_dim)
        return lax.cond(
            jnp.any(visible),
            lambda carried_in: attend_block(
                carried_in, query_heads, visible, split_pairs[:, :, 0], split_pairs[:, :, 1]
            ),
            lambda carried_in: carried_in,
            carried,
        )

    carried = start_state
    new_piece = lax.all_gather(pairs_new, "seq", axis=0, tiled=True)
    cache_piece = lax.all_gather(cache_lines, "seq", axis=0, tiled=True)
    piece_rows = new_piece.shape[0]
    stride = block_size(piece_rows)
    new_blocks = new_piece.reshape(piece_rows // stride, stride, -1)
    cache_blocks = cache_piece.reshape(piece_rows // stride, 2 * stride, kv_local, 2, head_dim)
    offsets = stride * jnp.arange(piece_rows // stride, dtype=jnp.int32)
    everything = jnp.ones((tokens_here, 2 * stride), bool)

    def visit(carried_in, block_part):
        new_block, cache_block, key_first = block_part
        carried_in = new_keys_part(carried_in, new_block, key_first)
        carried_in = lax.cond(
            holds_first,
            lambda inner: attend_block(
                inner, query_heads, everything, cache_block[:, :, 0], cache_block[:, :, 1]
            ),
            lambda inner: inner,
            carried_in,
        )
        return (carried_in, None)

    carried, _ = lax.scan(visit, carried, (new_blocks, cache_blocks, offsets))
    best_final, total_final, summed_final = carried
    attended = (
        (summed_final / total_final[..., None])
        .transpose(2, 0, 1, 3)
        .reshape(tokens_here, -1)
        .astype(jnp.bfloat16)
    )
    mixed_rows = lax.psum_scatter(
        jnp.dot(attended, o_weight, preferred_element_type=jnp.float32).astype(jnp.bfloat16),
        "exp",
        scatter_dimension=0,
        tiled=True,
    ).astype(jnp.float32)
    moe_rows = mixed_rows.shape[0]
    residual = (
        lax.dynamic_slice_in_dim(hidden_in, exp_index * moe_rows, moe_rows, 0).astype(jnp.float32)
        + residual_scale * mixed_rows
    )
    moe_in = rms_norm(residual, moe_gain)
    top_count = routes.shape[1]
    assigns = moe_rows * top_count
    capacity = 2 * moe_rows * top_count // EXPERTS
    flat_ids = routes.reshape(-1)
    hit_table = (flat_ids[:, None] == jnp.arange(EXPERTS, dtype=jnp.int32)[None, :]).astype(
        jnp.int32
    )
    earlier = jnp.cumsum(hit_table, axis=0) - hit_table
    slot_rank = jnp.sum(earlier * hit_table, axis=1)
    dest_slot = flat_ids * capacity + slot_rank
    source = (
        jnp.full((EXPERTS * capacity,), assigns, jnp.int32)
        .at[dest_slot]
        .set(jnp.arange(assigns, dtype=jnp.int32))
    )
    filled = source < assigns
    picked = moe_in[jnp.minimum(source, assigns - 1) // top_count]
    dispatched = jnp.where(filled[:, None], picked, jnp.zeros_like(picked)).reshape(
        seq_count, EXPERTS // seq_count, capacity, -1
    )
    hidden = jnp.einsum(
        "sexd,edf->sexf",
        lax.all_to_all(dispatched, "seq", split_axis=0, concat_axis=0, tiled=True),
        expert_in,
        preferred_element_type=jnp.float32,
    )
    half_width = hidden.shape[-1] // 2
    active = (jax.nn.silu(hidden[..., :half_width]) * hidden[..., half_width:]).astype(jnp.bfloat16)
    produced = jnp.einsum(
        "sexf,efd->sexd", active, expert_out, preferred_element_type=jnp.float32
    ).astype(jnp.bfloat16)
    returned = lax.all_to_all(produced, "seq", split_axis=0, concat_axis=0, tiled=True)
    flat_back = returned.reshape(EXPERTS * capacity, -1)
    per_assign = flat_back[dest_slot].reshape(moe_rows, top_count, -1)
    share = route_prob / jnp.sum(route_prob, axis=-1, keepdims=True)
    moe = jnp.sum(share[..., None] * per_assign.astype(jnp.float32), axis=1)
    hidden_out = (residual + residual_scale * moe).astype(jnp.bfloat16)
    return (hidden_out, page_rows)


def solution(mesh):
    return jax.shard_map(
        body,
        mesh=mesh,
        in_specs=(
            P("seq", None),
            P(),
            P(None, "exp"),
            P(None, "exp"),
            P(None, "exp"),
            P("exp", None),
            P("seq", "exp"),
            P(),
            P("seq", None, None),
            P("seq", None, None),
            P(("seq", "exp"), None),
            P(("seq", "exp"), None),
            P(),
        ),
        out_specs=(P(("seq", "exp"), None), P("seq", "exp", None, None)),
        check_vma=False,
    )
```

profile of v0, /device:TPU:0, one launch (start us, length us, event | category | flops | bytes accessed | tf_op | source)
XLA Modules:
  0.0 385.0 jit_solution(13722507623709581729)
XLA Ops:
  7.3 1.5 fusion.45
  8.8 1.7 convolution_convert_fusion.3
  10.5 1.7 convolution_convert_fusion.2
  14.7 40.6 %all-gather.3.cloned.1.call-done = bf16[2048,256]{0,1:T(8,128)(2,1)} async-done(((bf16[256,256]{0,1:T(8,128)(2,1)}), bf16[2048,256]{0,1:T(8,128)(2,1)}) %all-gather.3.cloned.1.call-update) | async-done | bytes 1048592 | tf_op jit(solution)/shard_map/all_gather | solution.py:134
  55.4 1.3 copy.142
  56.7 49.0 %all-gather.5.cloned.1.call-done = bf16[2048,512]{1,0:T(8,128)(2,1)} async-done(((bf16[256,512]{1,0:T(8,128)(2,1)}), bf16[2048,512]{1,0:T(8,128)(2,1)}) %all-gather.5.cloned.1.call-update) | async-done | bytes 2097168 | tf_op jit(solution)/shard_map/all_gather | solution.py:135
  105.7 8.9 %reshape.173 = bf16[4,1024,2,2,64]{4,3,2,1,0:T(2,128)(2,1)} reshape(bf16[2048,512]{1,0:T(8,128)(2,1)} %all-gather.5.cloned.1.call-done) | data formatting | bytes 4194304 | tf_op jit(solution)/shard_map/reshape | solution.py:139
  114.6 10.6 %copy.101 = bf16[4,1024,2,2,64]{1,4,2,3,0:T(8,128)(2,1)} copy(bf16[4,1024,2,2,64]{4,3,2,1,0:T(2,128)(2,1)} %reshape.173) | data formatting | bytes 4194304
  125.3 35.4 %while.16 = (s32[]{:T(128)}, f32[2,3,256]{2,1,0:T(4,128)S(1)}, f32[2,3,256]{2,1,0:T(4,128)S(1)}, f32[2,3,256,64]{2,3,1,0:T(8,128)S(1)}, pred[]{:T(512)}, /*index...) while((s32[]{:T(128)}, f32[2,3,256]{2,1,0:T(4,128)S(1)}, ...), condition=%wide.region_11.12_spmd.clone.clone, body=%wide.region_1.11_spmd.clone.clone.sunk | while | flops 627712256 | bytes 33374036 | solution.py:156
  129.0 2.5 conditional.8
  131.5 4.5 %conditional.9 = ((f32[2,3,256]{2,1,0:T(4,128)S(1)}, f32[2,3,256]{2,1,0:T(4,128)S(1)}, f32[2,3,256,64]{2,3,1,0:T(8,128)S(1)})) conditional(s32[]{:T(128)} %convert_element_type.152, (f32[2,3,256]{2,1,0:T(4,128)S(1)}, f32[2,3,256]{2,1,0:T(4,128)S(1)}, f32[2,3,256,64]{2,3,1,0:T(8,128)S(1)}) %get-tuple-element.445, ...), branch_computations={%region_7.7_spmd, %region_8.10_spmd} | conditional | flops 415435776 | bytes 21532708 | solution.py:146
  131.5 1.1 dynamic-slice_bitcast_fusion
  132.6 1.0 bitcast_reduce_fusion
  133.7 1.0 fusion.19
  134.7 1.2 fusion.22
  139.7 4.5 %conditional.9 = ((f32[2,3,256]{2,1,0:T(4,128)S(1)}, f32[2,3,256]{2,1,0:T(4,128)S(1)}, f32[2,3,256,64]{2,3,1,0:T(8,128)S(1)})) conditional(s32[]{:T(128)} %convert_element_type.152, (f32[2,3,256]{2,1,0:T(4,128)S(1)}, f32[2,3,256]{2,1,0:T(4,128)S(1)}, f32[2,3,256,64]{2,3,1,0:T(8,128)S(1)}) %get-tuple-element.445, ...), branch_computations={%region_7.7_spmd, %region_8.10_spmd} | conditional | flops 415435776 | bytes 21532708 | solution.py:146
  139.8 1.1 dynamic-slice_bitcast_fusion
  140.8 1.0 bitcast_reduce_fusion
  141.9 1.0 fusion.19
  143.0 1.2 fusion.22
  148.0 4.5 %conditional.9 = ((f32[2,3,256]{2,1,0:T(4,128)S(1)}, f32[2,3,256]{2,1,0:T(4,128)S(1)}, f32[2,3,256,64]{2,3,1,0:T(8,128)S(1)})) conditional(s32[]{:T(128)} %convert_element_type.152, (f32[2,3,256]{2,1,0:T(4,128)S(1)}, f32[2,3,256]{2,1,0:T(4,128)S(1)}, f32[2,3,256,64]{2,3,1,0:T(8,128)S(1)}) %get-tuple-element.445, ...), branch_computations={%region_7.7_spmd, %region_8.10_spmd} | conditional | flops 415435776 | bytes 21532708 | solution.py:146
  148.0 1.1 dynamic-slice_bitcast_fusion
  149.1 1.0 bitcast_reduce_fusion
  150.1 1.0 fusion.19
  151.2 1.2 fusion.22
  156.2 4.5 %conditional.9 = ((f32[2,3,256]{2,1,0:T(4,128)S(1)}, f32[2,3,256]{2,1,0:T(4,128)S(1)}, f32[2,3,256,64]{2,3,1,0:T(8,128)S(1)})) conditional(s32[]{:T(128)} %convert_element_type.152, (f32[2,3,256]{2,1,0:T(4,128)S(1)}, f32[2,3,256]{2,1,0:T(4,128)S(1)}, f32[2,3,256,64]{2,3,1,0:T(8,128)S(1)}) %get-tuple-element.445, ...), branch_computations={%region_7.7_spmd, %region_8.10_spmd} | conditional | flops 415435776 | bytes 21532708 | solution.py:146
  156.2 1.1 dynamic-slice_bitcast_fusion
  157.3 1.0 bitcast_reduce_fusion
  158.4 1.0 fusion.19
  159.4 1.2 fusion.22
  160.8 1.5 convolution_convert_fusion
  162.6 1.2 reduce-window.6
  164.3 2.4 scatter_custom_fusion
  166.9 19.4 %reduce-scatter.2.cloned.1.call-done = bf16[64,1536]{1,0:T(8,128)(2,1)} async-done(((bf16[256,1536]{1,0:T(8,128)(2,1)}), bf16[64,1536]{1,0:T(8,128)(2,1)}) %reduce-scatter.2.cloned.1.call-update) | async-done | bytes 196624 | tf_op jit(solution)/shard_map/reduce_scatter | solution.py:164
  186.3 1.1 multiply_reduce_fusion
  188.5 5.6 %gather_fusion = bf16[1024,1536]{1,0:T(8,128)(2,1)} fusion(bf16[64,1536]{1,0:T(8,128)(2,1)S(1)} %multiply_convert_fusion, s32[1024]{0:T(1024)S(1)} %fusion.59), kind=kCustom, calls=%fused_computation | custom fusion | bytes 6295552 | tf_op jit(solution)/shard_map/gather | solution.py:192
  194.1 3.8 broadcast_select_fusion
  197.9 5.8 %all-to-all-start = ((bf16[8,4,32,1536]{3,2,1,0:T(8,128)(2,1)}), bf16[8,4,32,1536]{3,2,1,0:T(8,128)(2,1)}, u32[]{:S(2)}, u32[]{:S(2)}) async-start(bf16[8,4,32,1536]{3,2,1,0:T(8,128)(2,1)} %broadcast_select_fusion), calls=%async_computation.1 | async-start | bytes 6291456 | tf_op jit(solution)/shard_map/all_to_all | solution.py:198
  204.9 69.6 %all-to-all-done = bf16[8,4,32,1536]{3,2,1,0:T(8,128)(2,1)} async-done(((bf16[8,4,32,1536]{3,2,1,0:T(8,128)(2,1)}), bf16[8,4,32,1536]{3,2,1,0:T(8,128)(2,1)}, u32[]{:S(2)}, u32[]{:S(2)}) %all-to-all-start) | async-done | bytes 3145760 | tf_op jit(solution)/shard_map/all_to_all | solution.py:198
  274.5 3.6 all-to-all-start.2
  278.2 7.4 %fusion.39 = f32[8,4,32,1024]{3,2,0,1:T(8,128)S(1)} fusion(bf16[4,1536,1024]{2,1,0:T(8,128)(2,1)} %param.27, bf16[8,4,32,1536]{3,2,1,0:T(8,128)(2,1)} %all-to-all-done), kind=kOutput, calls=%fused_computation.53 | convolution fusion | flops 3221225472 | bytes 19922944 | tf_op jit(solution)/shard_map/sexd,edf->sexf/dot_general | solution.py:196
  285.6 4.6 %fusion.34 = bf16[8,4,32,1536]{3,2,0,1:T(8,128)(2,1)S(1)} fusion(bf16[4,512,1536]{2,1,0:T(8,128)(2,1)} %param.28, f32[8,4,32,1024]{3,2,0,1:T(8,128)S(1)} %fusion.39), kind=kOutput, calls=%fused_computation.47 | convolution fusion | flops 1615331328 | bytes 13631488 | tf_op jit(solution)/shard_map/sexf,efd->sexd/dot_general | solution.py:204
  290.2 1.9 copy.108
  292.1 6.1 %all-to-all-start.1 = ((bf16[8,4,32,1536]{3,2,1,0:T(8,128)(2,1)}), bf16[8,4,32,1536]{3,2,1,0:T(8,128)(2,1)}, u32[]{:S(2)}, u32[]{:S(2)}) async-start(bf16[8,4,32,1536]{3,2,1,0:T(8,128)(2,1)} %copy.108), calls=%async_computation.2 | async-start | bytes 6291456 | tf_op jit(solution)/shard_map/all_to_all | solution.py:207
  301.4 67.3 %all-to-all-done.1 = bf16[8,4,32,1536]{3,2,1,0:T(8,128)(2,1)} async-done(((bf16[8,4,32,1536]{3,2,1,0:T(8,128)(2,1)}), bf16[8,4,32,1536]{3,2,1,0:T(8,128)(2,1)}, u32[]{:S(2)}, u32[]{:S(2)}) %all-to-all-start.1) | async-done | bytes 3145760 | tf_op jit(solution)/shard_map/all_to_all | solution.py:207
  368.7 5.9 %gather_fusion.1 = bf16[512,1536]{1,0:T(8,128)(2,1)S(1)} fusion(bf16[1024,1536]{1,0:T(8,128)(2,1)} %bitcast.33, s32[1024]{0:T(1024)S(1)} %pad_clamp_fusion), kind=kCustom, calls=%fused_computation.1 | custom fusion | bytes 3147776 | tf_op jit(solution)/shard_map/gather | solution.py:209
  374.6 2.2 fusion.37
  376.8 1.7 add_convert_fusion
  (123 shorter events, 23.4 us)
Async XLA Ops:
  7.2 153.6 %copy-start = (bf16[384,1536]{1,0:T(8,128)(2,1)S(1)}, bf16[384,1536]{1,0:T(8,128)(2,1)}, u32[]{:S(2)}) copy-start(bf16[384,1536]{1,0:T(8,128)(2,1)} %param.24) | copy-start | bytes 3538948
  7.2 6.7 %copy-start.1 = (bf16[256,1536]{1,0:T(8,128)(2,1)S(1)}, bf16[256,1536]{1,0:T(8,128)(2,1)}, u32[]{:S(2)}) copy-start(bf16[256,1536]{1,0:T(8,128)(2,1)} %param.19) | copy-start | bytes 2359300
  7.2 6.7 %copy-start.10 = (f32[1536]{0:T(1024)S(1)}, f32[1536]{0:T(1024)}, u32[]{:S(2)}) copy-start(f32[1536]{0:T(1024)} %param.20) | copy-start | bytes 18436
  7.2 5.8 %copy-start.4 = (bf16[512,256]{1,0:T(8,128)(2,1)S(1)}, bf16[512,256]{1,0:T(8,128)(2,1)}, u32[]{:S(2)}) copy-start(bf16[512,256]{1,0:T(8,128)(2,1)} %param.25) | copy-start | bytes 786436
  7.2 6.7 %copy-start.9 = (bf16[1536,384]{1,0:T(8,128)(2,1)S(1)}, bf16[1536,384]{1,0:T(8,128)(2,1)}, u32[]{:S(2)}) copy-start(bf16[1536,384]{1,0:T(8,128)(2,1)} %param.21) | copy-start | bytes 3538948
  7.2 48.1 %all-gather.3.cloned.1.call-start = ((), (), s32[]{:S(2)}) async-start(), calls=%async_computation.4 | async-start | bytes 1179648 | tf_op jit(solution)/shard_map/all_gather | solution.py:134
  13.0 92.7 %all-gather.5.cloned.1.call-start = ((), (), s32[]{:S(2)}) async-start(), calls=%async_computation.5 | async-start | bytes 2359296 | tf_op jit(solution)/shard_map/all_gather | solution.py:135
  13.9 172.4 %reduce-scatter.2.cloned.1.call-start = ((), (), s32[]{:S(2)}) async-start(), calls=%async_computation.6 | async-start | bytes 983040 | tf_op jit(solution)/shard_map/reduce_scatter | solution.py:164
  160.7 1.6 copy-start.5
  160.7 25.6 %copy-start.2 = (bf16[256,1536]{1,0:T(8,128)(2,1)S(1)}, bf16[256,1536]{1,0:T(8,128)(2,1)}, u32[]{:S(2)}) copy-start(bf16[256,1536]{1,0:T(8,128)(2,1)} %param.19) | copy-start | bytes 2359300
  160.7 26.7 %copy-start.7 = (f32[1536]{0:T(1024)S(1)}, f32[1536]{0:T(1024)}, u32[]{:S(2)}) copy-start(f32[1536]{0:T(1024)} %param.26) | copy-start | bytes 18436
  197.9 5.8 %copy-start.3 = (bf16[256,2,2,64]{0,3,2,1:T(8,128)(2,1)S(1)}, bf16[256,2,2,64]{0,3,2,1:T(8,128)(2,1)}, u32[]{:S(2)}) copy-start(bf16[256,2,2,64]{0,3,2,1:T(8,128)(2,1)} %pad_maximum_fusion) | copy-start | bytes 393220
  197.9 76.6 %all-to-all-start = ((bf16[8,4,32,1536]{3,2,1,0:T(8,128)(2,1)}), bf16[8,4,32,1536]{3,2,1,0:T(8,128)(2,1)}, u32[]{:S(2)}, u32[]{:S(2)}) async-start(bf16[8,4,32,1536]{3,2,1,0:T(8,128)(2,1)} %broadcast_select_fusion), calls=%async_computation.1 | async-start | bytes 6291456 | tf_op jit(solution)/shard_map/all_to_all | solution.py:198
  274.5 17.6 %all-to-all-start.2 = ((bf16[4,8,2048]{2,0,1:T(4,128)(2,1)}), bf16[4,8,2048]{2,0,1:T(4,128)(2,1)S(1)}, u32[]{:S(2)}, u32[]{:S(2)}) async-start(bf16[4,8,2048]{2,0,1:T(4,128)(2,1)} %copy.110), calls=%async_computation.3 | async-start | bytes 262144 | tf_op jit(solution)/shard_map/all_to_all | solution.py:92
  292.1 6.1 %copy-start.6 = (f32[64,8]{0,1:T(8,128)S(1)}, f32[64,8]{0,1:T(8,128)}, u32[]{:S(2)}) copy-start(f32[64,8]{0,1:T(8,128)} %param.30) | copy-start | bytes 6148
  292.1 7.1 %copy-start.8 = (s32[256]{0:T(256)S(1)}, s32[256]{0:T(256)}, u32[]{:S(2)}) copy-start(s32[256]{0:T(256)} %param.31) | copy-start | bytes 3076
  292.1 76.6 %all-to-all-start.1 = ((bf16[8,4,32,1536]{3,2,1,0:T(8,128)(2,1)}), bf16[8,4,32,1536]{3,2,1,0:T(8,128)(2,1)}, u32[]{:S(2)}, u32[]{:S(2)}) async-start(bf16[8,4,32,1536]{3,2,1,0:T(8,128)(2,1)} %copy.108), calls=%async_computation.2 | async-start | bytes 6291456 | tf_op jit(solution)/shard_map/all_to_all | solution.py:207
Sparse Core Ops, SparseCore 0:
  13.1 42.2 all-gather.2
  57.5 48.1 all-gather.4
  162.4 23.8 reduce-scatter.1
where the time goes:
time: 386 us; the launch traced here: 385 us
  waiting for transfers between devices  246 us (64%)
  local copies, waits for them, and re-layouts  49.6 us (13%)
  matrix products  28.3 us (7%)
  other arithmetic  28.1 us (7%)
  starting transfers between devices  15.7 us (4%)
  between operations  14.1 us (4%)
    all_to_all x1, waiting for transfers between devices, body(): lax.all_to_all(dispatched, 'seq', split_axis=0, concat_axis=0, tiled=True)  69.6 us
    all_to_all x1, waiting for transfers between devices, body(): lax.all_to_all(produced, 'seq', split_axis=0, concat_axis=0, tiled=True)  67.3 us
    all_gather x1, waiting for transfers between devices, body(): cache_piece = lax.all_gather(cache_lines, 'seq', axis=0, tiled=True)  49 us
    all_gather x1, waiting for transfers between devices, body(): new_piece = lax.all_gather(pairs_new, 'seq', axis=0, tiled=True)  40.6 us
    reduce_scatter x1, waiting for transfers between devices, body(): lax.psum_scatter(jnp.dot(attended, o_weight, preferred_element_type=jnp.f...  19.4 us
    unnamed x26, local copies, waits for them, and re-layouts  11.7 us
    reshape x1, local copies, waits for them, and re-layouts, body(): cache_piece.reshape(piece_rows // stride, 2 * stride, kv_local, 2, head_dim)  8.88 us
  transfers between devices with their start and end apart: 6, of which 5 were waited for; matrix products, arithmetic and copies ran while one was open for 7% of the time, Pallas kernels for 0%

commit v1 on v0

--- a/solution.py
+++ b/solution.py
@@ -131,8 +131,13 @@
         )
 
     carried = start_state
-    new_piece = lax.all_gather(pairs_new, "seq", axis=0, tiled=True)
-    cache_piece = lax.all_gather(cache_lines, "seq", axis=0, tiled=True)
+    new_piece, cache_piece = jnp.split(
+        lax.all_gather(
+            jnp.concatenate([pairs_new, cache_lines], axis=1), "seq", axis=0, tiled=True
+        ),
+        [pairs_new.shape[1]],
+        axis=1,
+    )
     piece_rows = new_piece.shape[0]
     stride = block_size(piece_rows)
     new_blocks = new_piece.reshape(piece_rows // stride, stride, -1)

time: 386 us -> 354 us (0.917)
  waiting for transfers between devices: 246 us -> 217 us
  local copies, waits for them, and re-layouts: 49.6 us -> 44.6 us
    all_gather x2 -> x1, waiting for transfers between devices: 89.6 us -> 61.2 us  [body(): lax.all_gather(jnp.concatenate([pairs_new, cache_lines], axis=1), 'seq',...]
    reshape x1, local copies, waits for them, and re-layouts: 8.88 us -> 3.64 us  [body(): cache_piece.reshape(piece_rows // stride, 2 * stride, kv_local, 2, head_dim)]
  transfers between devices with their start and end apart: 6 -> 5, of which waited for: 5 -> 4; matrix products, arithmetic and copies ran while one was open for 7% -> 7% of each run, Pallas kernels for 0% -> 0%
where the time goes in v1:
time: 354 us; the launch traced here: 353 us
  waiting for transfers between devices  217 us (61%)
  local copies, waits for them, and re-layouts  44.6 us (13%)
  matrix products  29.5 us (8%)
  other arithmetic  28.2 us (8%)
  starting transfers between devices  15.5 us (4%)
  between operations  14.4 us (4%)
    all_to_all x1, waiting for transfers between devices, body(): lax.all_to_all(dispatched, 'seq', split_axis=0, concat_axis=0, tiled=True)  69.6 us
    all_to_all x1, waiting for transfers between devices, body(): lax.all_to_all(produced, 'seq', split_axis=0, concat_axis=0, tiled=True)  67.3 us
    all_gather x1, waiting for transfers between devices, body(): lax.all_gather(jnp.concatenate([pairs_new, cache_lines], axis=1), 'seq',...  61.2 us
    reduce_scatter x1, waiting for transfers between devices, body(): lax.psum_scatter(jnp.dot(attended, o_weight, preferred_element_type=jnp.f...  19.4 us
    unnamed x26, local copies, waits for them, and re-layouts  11.8 us
    dot_general x1, matrix products, body(): jnp.einsum('sexd,edf->sexf', lax.all_to_all(dispatched, 'seq', split_axis...  7.35 us
  transfers between devices with their start and end apart: 5, of which 4 were waited for; matrix products, arithmetic and copies ran while one was open for 7% of the time, Pallas kernels for 0%

profile of v1, /device:TPU:0, one launch (start us, length us, event | category | flops | bytes accessed | tf_op | source)
XLA Modules:
  0.0 353.1 jit_solution(13614838724813605585)
XLA Ops:
  7.3 1.5 fusion.45
  8.8 1.7 convolution_convert_fusion.3
  10.5 1.7 convolution_convert_fusion.2
  13.4 1.9 convolution_convert_fusion.1
  15.5 61.2 %all-gather.2.cloned.1.call-done = bf16[2048,768]{1,0:T(8,128)(2,1)} async-done(((bf16[256,768]{1,0:T(8,128)(2,1)}), bf16[2048,768]{1,0:T(8,128)(2,1)}) %all-gather.2.cloned.1.call-update) | async-done | bytes 3145744 | tf_op jit(solution)/shard_map/all_gather | solution.py:135
  76.6 1.6 slice-done
  78.2 3.6 %reshape.173 = bf16[4,1024,2,2,64]{4,3,2,1,0:T(2,128)(2,1)} reshape(bf16[2048,512]{1,0:T(8,128)(2,1)S(1)} %slice-done) | data formatting | bytes 4194304 | tf_op jit(solution)/shard_map/reshape | solution.py:144
  81.8 10.7 %copy.105 = bf16[4,1024,2,2,64]{1,4,2,3,0:T(8,128)(2,1)} copy(bf16[4,1024,2,2,64]{4,3,2,1,0:T(2,128)(2,1)} %reshape.173) | data formatting | bytes 4194304
  92.6 36.0 %while.16 = (s32[]{:T(128)}, f32[2,3,256]{2,1,0:T(4,128)S(1)}, f32[2,3,256]{2,1,0:T(4,128)S(1)}, f32[2,3,256,64]{2,3,1,0:T(8,128)S(1)}, pred[]{:T(512)}, /*index...) while((s32[]{:T(128)}, f32[2,3,256]{2,1,0:T(4,128)S(1)}, ...), condition=%wide.region_11.12_spmd.clone.clone, body=%wide.region_1.11_spmd.clone.clone.sunk | while | flops 627712256 | bytes 33898324 | solution.py:161
  96.5 2.5 conditional.8
  99.0 4.5 %conditional.9 = ((f32[2,3,256]{2,1,0:T(4,128)S(1)}, f32[2,3,256]{2,1,0:T(4,128)S(1)}, f32[2,3,256,64]{2,3,1,0:T(8,128)S(1)})) conditional(s32[]{:T(128)} %convert_element_type.152, (f32[2,3,256]{2,1,0:T(4,128)S(1)}, f32[2,3,256]{2,1,0:T(4,128)S(1)}, f32[2,3,256,64]{2,3,1,0:T(8,128)S(1)}) %get-tuple-element.445, ...), branch_computations={%region_7.7_spmd, %region_8.10_spmd} | conditional | flops 415435776 | bytes 21532708 | solution.py:151
  99.1 1.1 dynamic-slice_bitcast_fusion
  100.1 1.0 bitcast_reduce_fusion
  101.2 1.0 fusion.19
  102.3 1.2 fusion.22
  107.4 4.5 %conditional.9 = ((f32[2,3,256]{2,1,0:T(4,128)S(1)}, f32[2,3,256]{2,1,0:T(4,128)S(1)}, f32[2,3,256,64]{2,3,1,0:T(8,128)S(1)})) conditional(s32[]{:T(128)} %convert_element_type.152, (f32[2,3,256]{2,1,0:T(4,128)S(1)}, f32[2,3,256]{2,1,0:T(4,128)S(1)}, f32[2,3,256,64]{2,3,1,0:T(8,128)S(1)}) %get-tuple-element.445, ...), branch_computations={%region_7.7_spmd, %region_8.10_spmd} | conditional | flops 415435776 | bytes 21532708 | solution.py:151
  107.4 1.1 dynamic-slice_bitcast_fusion
  108.5 1.0 bitcast_reduce_fusion
  109.6 1.0 fusion.19
  110.6 1.2 fusion.22
  115.8 4.5 %conditional.9 = ((f32[2,3,256]{2,1,0:T(4,128)S(1)}, f32[2,3,256]{2,1,0:T(4,128)S(1)}, f32[2,3,256,64]{2,3,1,0:T(8,128)S(1)})) conditional(s32[]{:T(128)} %convert_element_type.152, (f32[2,3,256]{2,1,0:T(4,128)S(1)}, f32[2,3,256]{2,1,0:T(4,128)S(1)}, f32[2,3,256,64]{2,3,1,0:T(8,128)S(1)}) %get-tuple-element.445, ...), branch_computations={%region_7.7_spmd, %region_8.10_spmd} | conditional | flops 415435776 | bytes 21532708 | solution.py:151
  115.8 1.1 dynamic-slice_bitcast_fusion
  116.9 1.0 bitcast_reduce_fusion
  118.0 1.0 fusion.19
  119.0 1.2 fusion.22
  124.2 4.5 %conditional.9 = ((f32[2,3,256]{2,1,0:T(4,128)S(1)}, f32[2,3,256]{2,1,0:T(4,128)S(1)}, f32[2,3,256,64]{2,3,1,0:T(8,128)S(1)})) conditional(s32[]{:T(128)} %convert_element_type.152, (f32[2,3,256]{2,1,0:T(4,128)S(1)}, f32[2,3,256]{2,1,0:T(4,128)S(1)}, f32[2,3,256,64]{2,3,1,0:T(8,128)S(1)}) %get-tuple-element.445, ...), branch_computations={%region_7.7_spmd, %region_8.10_spmd} | conditional | flops 415435776 | bytes 21532708 | solution.py:151
  124.2 1.1 dynamic-slice_bitcast_fusion
  126.3 1.0 fusion.19
  127.4 1.2 fusion.22
  128.8 1.5 convolution_convert_fusion
  130.6 1.2 reduce-window.6
  132.3 2.4 scatter_custom_fusion
  134.9 19.4 %reduce-scatter.2.cloned.1.call-done = bf16[64,1536]{1,0:T(8,128)(2,1)} async-done(((bf16[256,1536]{1,0:T(8,128)(2,1)}), bf16[64,1536]{1,0:T(8,128)(2,1)}) %reduce-scatter.2.cloned.1.call-update) | async-done | bytes 196624 | tf_op jit(solution)/shard_map/reduce_scatter | solution.py:169
  154.2 1.1 multiply_reduce_fusion
  155.4 1.0 multiply_convert_fusion
  156.4 5.6 %gather_fusion = bf16[1024,1536]{1,0:T(8,128)(2,1)} fusion(bf16[64,1536]{1,0:T(8,128)(2,1)S(1)} %multiply_convert_fusion, s32[1024]{0:T(1024)S(1)} %fusion.59), kind=kCustom, calls=%fused_computation | custom fusion | bytes 6295552 | tf_op jit(solution)/shard_map/gather | solution.py:197
  162.0 3.8 %broadcast_select_fusion = bf16[8,4,32,1536]{3,2,1,0:T(8,128)(2,1)} fusion(bf16[8,4,32,1536]{3,2,1,0:T(8,128)(2,1)} %bitcast.138, pred[8,4,32]{2,1,0:T(4,128)(4,1)S(1)} %broadcast_in_dim.86), kind=kLoop, calls=%fused_computation.51 | loop fusion | flops 1572864 | bytes 6292480 | tf_op jit(solution)/shard_map/jit(_where)/select_n | solution.py:198
  165.8 5.7 %all-to-all-start = ((bf16[8,4,32,1536]{3,2,1,0:T(8,128)(2,1)}), bf16[8,4,32,1536]{3,2,1,0:T(8,128)(2,1)}, u32[]{:S(2)}, u32[]{:S(2)}) async-start(bf16[8,4,32,1536]{3,2,1,0:T(8,128)(2,1)} %broadcast_select_fusion), calls=%async_computation.1 | async-start | bytes 6291456 | tf_op jit(solution)/shard_map/all_to_all | solution.py:203
  172.7 69.6 %all-to-all-done = bf16[8,4,32,1536]{3,2,1,0:T(8,128)(2,1)} async-done(((bf16[8,4,32,1536]{3,2,1,0:T(8,128)(2,1)}), bf16[8,4,32,1536]{3,2,1,0:T(8,128)(2,1)}, u32[]{:S(2)}, u32[]{:S(2)}) %all-to-all-start) | async-done | bytes 3145760 | tf_op jit(solution)/shard_map/all_to_all | solution.py:203
  242.3 3.6 %all-to-all-start.2 = ((bf16[4,8,2048]{2,0,1:T(4,128)(2,1)}), bf16[4,8,2048]{2,0,1:T(4,128)(2,1)S(1)}, u32[]{:S(2)}, u32[]{:S(2)}) async-start(bf16[4,8,2048]{2,0,1:T(4,128)(2,1)} %copy.114), calls=%async_computation.3 | async-start | bytes 262144 | tf_op jit(solution)/shard_map/all_to_all | solution.py:92
  245.9 7.4 %fusion.39 = f32[8,4,32,1024]{3,2,0,1:T(8,128)S(1)} fusion(bf16[4,1536,1024]{2,1,0:T(8,128)(2,1)} %param.27, bf16[8,4,32,1536]{3,2,1,0:T(8,128)(2,1)} %all-to-all-done), kind=kOutput, calls=%fused_computation.53 | convolution fusion | flops 3221225472 | bytes 19922944 | tf_op jit(solution)/shard_map/sexd,edf->sexf/dot_general | solution.py:201
  253.3 4.6 %fusion.34 = bf16[8,4,32,1536]{3,2,0,1:T(8,128)(2,1)S(1)} fusion(bf16[4,512,1536]{2,1,0:T(8,128)(2,1)} %param.28, f32[8,4,32,1024]{3,2,0,1:T(8,128)S(1)} %fusion.39), kind=kOutput, calls=%fused_computation.47 | convolution fusion | flops 1615331328 | bytes 13631488 | tf_op jit(solution)/shard_map/sexf,efd->sexd/dot_general | solution.py:209
  257.9 1.9 copy.112
  259.9 6.1 %all-to-all-start.1 = ((bf16[8,4,32,1536]{3,2,1,0:T(8,128)(2,1)}), bf16[8,4,32,1536]{3,2,1,0:T(8,128)(2,1)}, u32[]{:S(2)}, u32[]{:S(2)}) async-start(bf16[8,4,32,1536]{3,2,1,0:T(8,128)(2,1)} %copy.112), calls=%async_computation.2 | async-start | bytes 6291456 | tf_op jit(solution)/shard_map/all_to_all | solution.py:212
  269.1 67.3 %all-to-all-done.1 = bf16[8,4,32,1536]{3,2,1,0:T(8,128)(2,1)} async-done(((bf16[8,4,32,1536]{3,2,1,0:T(8,128)(2,1)}), bf16[8,4,32,1536]{3,2,1,0:T(8,128)(2,1)}, u32[]{:S(2)}, u32[]{:S(2)}) %all-to-all-start.1) | async-done | bytes 3145760 | tf_op jit(solution)/shard_map/all_to_all | solution.py:212
  336.4 5.9 %gather_fusion.1 = bf16[512,1536]{1,0:T(8,128)(2,1)S(1)} fusion(bf16[1024,1536]{1,0:T(8,128)(2,1)} %bitcast.34, s32[1024]{0:T(1024)S(1)} %pad_clamp_fusion), kind=kCustom, calls=%fused_computation.1 | custom fusion | bytes 3147776 | tf_op jit(solution)/shard_map/gather | solution.py:214
  342.3 2.2 fusion.37
  344.5 1.7 add_convert_fusion
  (129 shorter events, 22.8 us)
Async XLA Ops:
  7.2 121.6 %copy-start = (bf16[384,1536]{1,0:T(8,128)(2,1)S(1)}, bf16[384,1536]{1,0:T(8,128)(2,1)}, u32[]{:S(2)}) copy-start(bf16[384,1536]{1,0:T(8,128)(2,1)} %param.24) | copy-start | bytes 3538948
  7.2 6.2 %copy-start.1 = (bf16[256,1536]{1,0:T(8,128)(2,1)S(1)}, bf16[256,1536]{1,0:T(8,128)(2,1)}, u32[]{:S(2)}) copy-start(bf16[256,1536]{1,0:T(8,128)(2,1)} %param.19) | copy-start | bytes 2359300
  7.2 6.2 %copy-start.10 = (f32[1536]{0:T(1024)S(1)}, f32[1536]{0:T(1024)}, u32[]{:S(2)}) copy-start(f32[1536]{0:T(1024)} %param.20) | copy-start | bytes 18436
  7.2 5.2 %copy-start.5 = (bf16[512,256]{1,0:T(8,128)(2,1)S(1)}, bf16[512,256]{1,0:T(8,128)(2,1)}, u32[]{:S(2)}) copy-start(bf16[512,256]{1,0:T(8,128)(2,1)} %param.25) | copy-start | bytes 786436
  7.2 69.4 %all-gather.2.cloned.1.call-start = ((), (), s32[]{:S(2)}) async-start(), calls=%async_computation.4 | async-start | bytes 3538944 | tf_op jit(solution)/shard_map/all_gather | solution.py:135
  12.3 3.2 copy-start.3
  13.3 140.9 %reduce-scatter.2.cloned.1.call-start = ((), (), s32[]{:S(2)}) async-start(), calls=%async_computation.5 | async-start | bytes 983040 | tf_op jit(solution)/shard_map/reduce_scatter | solution.py:169
  76.6 1.6 slice-start
  81.8 10.8 %slice-start.1 = ((bf16[2048,768]{1,0:T(8,128)(2,1)}), bf16[2048,256]{1,0:T(8,128)(2,1)S(1)}, s32[]{:S(2)}) async-start(bf16[2048,768]{1,0:T(8,128)(2,1)} %all-gather.2.cloned.1.call-done), calls=%async_computation.7 | async-start | bytes 2097152 | tf_op jit(solution)/shard_map/split | solution.py:134
  128.7 1.6 copy-start.6
  128.7 25.6 %copy-start.2 = (bf16[256,1536]{1,0:T(8,128)(2,1)S(1)}, bf16[256,1536]{1,0:T(8,128)(2,1)}, u32[]{:S(2)}) copy-start(bf16[256,1536]{1,0:T(8,128)(2,1)} %param.19) | copy-start | bytes 2359300
  128.7 26.7 %copy-start.8 = (f32[1536]{0:T(1024)S(1)}, f32[1536]{0:T(1024)}, u32[]{:S(2)}) copy-start(f32[1536]{0:T(1024)} %param.26) | copy-start | bytes 18436
  165.8 5.7 %copy-start.4 = (bf16[256,2,2,64]{0,3,2,1:T(8,128)(2,1)S(1)}, bf16[256,2,2,64]{0,3,2,1:T(8,128)(2,1)}, u32[]{:S(2)}) copy-start(bf16[256,2,2,64]{0,3,2,1:T(8,128)(2,1)} %copy-done.3) | copy-start | bytes 393220
  165.8 76.5 %all-to-all-start = ((bf16[8,4,32,1536]{3,2,1,0:T(8,128)(2,1)}), bf16[8,4,32,1536]{3,2,1,0:T(8,128)(2,1)}, u32[]{:S(2)}, u32[]{:S(2)}) async-start(bf16[8,4,32,1536]{3,2,1,0:T(8,128)(2,1)} %broadcast_select_fusion), calls=%async_computation.1 | async-start | bytes 6291456 | tf_op jit(solution)/shard_map/all_to_all | solution.py:203
  242.3 17.5 %all-to-all-start.2 = ((bf16[4,8,2048]{2,0,1:T(4,128)(2,1)}), bf16[4,8,2048]{2,0,1:T(4,128)(2,1)S(1)}, u32[]{:S(2)}, u32[]{:S(2)}) async-start(bf16[4,8,2048]{2,0,1:T(4,128)(2,1)} %copy.114), calls=%async_computation.3 | async-start | bytes 262144 | tf_op jit(solution)/shard_map/all_to_all | solution.py:92
  259.8 6.1 %copy-start.7 = (f32[64,8]{0,1:T(8,128)S(1)}, f32[64,8]{0,1:T(8,128)}, u32[]{:S(2)}) copy-start(f32[64,8]{0,1:T(8,128)} %param.30) | copy-start | bytes 6148
  259.8 7.1 %copy-start.9 = (s32[256]{0:T(256)S(1)}, s32[256]{0:T(256)}, u32[]{:S(2)}) copy-start(s32[256]{0:T(256)} %param.31) | copy-start | bytes 3076
  259.9 76.6 %all-to-all-start.1 = ((bf16[8,4,32,1536]{3,2,1,0:T(8,128)(2,1)}), bf16[8,4,32,1536]{3,2,1,0:T(8,128)(2,1)}, u32[]{:S(2)}, u32[]{:S(2)}) async-start(bf16[8,4,32,1536]{3,2,1,0:T(8,128)(2,1)} %copy.112), calls=%async_computation.2 | async-start | bytes 6291456 | tf_op jit(solution)/shard_map/all_to_all | solution.py:212
Sparse Core Ops, SparseCore 0:
  13.4 63.1 all-gather.1
  130.4 23.8 reduce-scatter.1
